TPU v7x, 128 devices: a whole 4x4x4 slice. The times are simulated.
128 devices in a mesh: expert: 8 (over z, core), ffn: 16 (over x, y).
Axes of the slice: x: 4, y: 4, z: 4, core: 2. Of those that a mesh axis runs over, the one named last changes fastest.
Arguments:
- queries: bfloat16 [512, 4096], P(('expert', 'ffn')), may hold values from -8 to 8
- new_keys: bfloat16 [512, 1024], P(('expert', 'ffn')), may hold values from -4 to 4
- new_values: bfloat16 [512, 1024], P(('expert', 'ffn')), may hold values from -5 to 5
- key_cache: bfloat16 [512, 512, 1024], P(('expert', 'ffn')), may hold values from -4 to 4
- value_cache: bfloat16 [512, 512, 1024], P(('expert', 'ffn')), may hold values from -5 to 5
- lengths: int32 [512], P(('expert', 'ffn')), may hold values from 1 to 512, 65536 in all
- residual: bfloat16 [512, 4096], P('expert', 'ffn'), may hold values from -16 to 16
- out_weight: bfloat16 [4096, 4096], P(None, 'ffn'), may hold values from -0.1875 to 0.1875
- norm_gain: float32 [4096], P('ffn'), may hold values from 0.25 to 1.75
- router: float32 [4096, 8], P('ffn'), may hold values from -0.09375 to 0.09375
- gate_weight: bfloat16 [8, 4096, 8192], P('expert', None, 'ffn'), may hold values from -0.09375 to 0.09375
- up_weight: bfloat16 [8, 4096, 8192], P('expert', None, 'ffn'), may hold values from -0.09375 to 0.09375
- down_weight: bfloat16 [8, 8192, 4096], P('expert', 'ffn'), may hold values from -0.09375 to 0.09375
- routes: int32 [512, 2], P('expert'), may hold values from 0 to 7, all different within a row; in each aligned block of 64 rows (0 to 63, 64 to 127, ...) at most 32 rows name the same one
Outputs:
- layer_out: bfloat16 [512, 4096], P('expert', 'ffn')
Inputs may be any that keep to these rules, and one draw needn't show every extreme that they name: The lengths of all 512 requests sum to 65536, and some request has exactly 512. `routes`: A request names two different experts. In each aligned block of 64 requests (the requests of one index of expert) no expert is named by more than 32 requests, a bound that some block reaches.
All inputs are finite; a program needn't handle non-finite values. No bound on the sum of `lengths` on one device may be relied on, other than what follows from the above.
Results may differ from a plain program's by a relative error of at most 0.0065.
Values may be sent and summed in bfloat16 or wider, within the bound.
No kernel may reach another device: no remote copies, remote signals or barrier semaphores. Data moves between devices by JAX's collectives and lax.ppermute only.
A program may use at most 128 MiB of HBM per device.

v0:
```python
import math
import jax
import jax.numpy as jnp
from jax import lax
from jax.sharding import PartitionSpec as P

D = 4096
QH = 32
KVH = 8
HD = 128
CACHE = 512
EPSILON = 1e-05
FLOOR = -1e30


def attend_local(queries, new_keys, new_values, key_cache, value_cache, lengths):
    request_count = queries.shape[0]
    group_size = QH // KVH
    score_scale = 1.0 / math.sqrt(HD)
    block_size = math.gcd(CACHE, 256)
    query_heads = queries.reshape(request_count, KVH, group_size, HD)
    key_view = key_cache.reshape(request_count, CACHE, KVH, HD)
    value_view = value_cache.reshape(request_count, CACHE, KVH, HD)
    score_new = (
        jnp.einsum(
            "rkgd,rkd->rkg",
            query_heads,
            new_keys.reshape(request_count, KVH, HD),
            preferred_element_type=jnp.float32,
        )
        * score_scale
    )
    value_start = jnp.broadcast_to(
        new_values.reshape(request_count, KVH, 1, HD).astype(jnp.float32),
        (request_count, KVH, group_size, HD),
    )
    initial = (score_new, jnp.ones_like(score_new), value_start)

    def block_step(block_index, carried):
        running_max, running_den, running_tot = carried
        offset = block_index * block_size
        keys_part = lax.dynamic_slice_in_dim(key_view, offset, block_size, 1)
        values_part = lax.dynamic_slice_in_dim(value_view, offset, block_size, 1)
        scores = (
            jnp.einsum(
                "rkgd,rpkd->rkgp", query_heads, keys_part, preferred_element_type=jnp.float32
            )
            * score_scale
        )
        positions = offset + jnp.arange(block_size, dtype=jnp.int32)
        live_mask = (positions[None, :] < lengths[:, None])[:, None, None, :]
        masked = jnp.where(live_mask, scores, FLOOR)
        new_max = jnp.maximum(running_max, jnp.max(masked, axis=-1))
        weights = jnp.where(live_mask, jnp.exp(masked - new_max[..., None]), 0.0)
        shrink = jnp.exp(running_max - new_max)
        new_den = running_den * shrink + jnp.sum(weights, axis=-1)
        new_tot = running_tot * shrink[..., None] + jnp.einsum(
            "rkgp,rpkd->rkgd",
            weights.astype(jnp.bfloat16),
            values_part,
            preferred_element_type=jnp.float32,
        )
        return (new_max, new_den, new_tot)

    block_total = (jnp.max(lengths) + block_size - 1) // block_size
    final_max, final_den, final_tot = lax.fori_loop(0, block_total, block_step, initial)
    return (final_tot / final_den[..., None]).astype(jnp.bfloat16).reshape(request_count, QH * HD)


def local(
    queries,
    new_keys,
    new_values,
    key_cache,
    value_cache,
    lengths,
    residual,
    out_weight,
    norm_gain,
    router,
    gate_weight,
    up_weight,
    down_weight,
    routes,
):
    attended = attend_local(queries, new_keys, new_values, key_cache, value_cache, lengths)
    hidden = residual.astype(jnp.float32) + jnp.dot(
        lax.all_gather(attended, "ffn", axis=0, tiled=True),
        out_weight,
        preferred_element_type=jnp.float32,
    )
    scaled = hidden * norm_gain
    square_part = jnp.sum(hidden * hidden, axis=-1)
    square_sum = lax.psum(square_part, "ffn")
    inverse = lax.rsqrt(square_sum / D + EPSILON)[:, None]
    logits = lax.psum(jnp.dot(scaled * inverse, router, precision=lax.Precision.HIGHEST), "ffn")
    normed = (scaled * inverse).astype(jnp.bfloat16)
    expert_count = lax.axis_size("expert")
    row_count = routes.shape[0]
    capacity = row_count // 2
    expert_ids = jnp.arange(expert_count, dtype=jnp.int32)
    chosen = routes[:, :, None] == expert_ids[None, None, :]
    picked = jnp.sum(jnp.where(chosen, logits[:, None, :], 0.0), axis=-1)
    first_weight = jax.nn.sigmoid(picked[:, 0] - picked[:, 1])
    route_weights = jnp.stack([first_weight, 1.0 - first_weight], axis=1)
    flat_hits = chosen.astype(jnp.int32).reshape(row_count * 2, expert_count)
    earlier = jnp.cumsum(flat_hits, axis=0) - flat_hits
    slots = jnp.sum(earlier * flat_hits, axis=-1).reshape(row_count, 2)
    targets = routes * capacity + slots
    slot_ids = jnp.arange(expert_count * capacity, dtype=jnp.int32)
    slot_hits = slot_ids[:, None, None] == targets[None, :, :]
    dispatch = jnp.sum(slot_hits.astype(jnp.float32), axis=-1).astype(jnp.bfloat16)
    combine = jnp.sum(jnp.where(slot_hits, route_weights[None, :, :], 0.0), axis=-1).T
    gate_local = gate_weight[0]
    up_local = up_weight[0]
    down_local = down_weight[0]
    share_rows = (
        jnp.dot(dispatch, normed, preferred_element_type=jnp.float32)
        .astype(jnp.bfloat16)
        .reshape(expert_count, capacity, normed.shape[1])
    )
    part_rows = lax.all_gather(
        lax.all_to_all(share_rows, "expert", split_axis=0, concat_axis=0, tiled=True),
        "ffn",
        axis=2,
        tiled=True,
    )
    gate_next = jnp.einsum("eck,kf->ecf", part_rows, gate_local, preferred_element_type=jnp.float32)
    up_next = jnp.einsum("eck,kf->ecf", part_rows, up_local, preferred_element_type=jnp.float32)
    inner = (jax.nn.silu(gate_next) * up_next).astype(jnp.bfloat16)
    partial_out = jnp.einsum("ecf,fd->ecd", inner, down_local, preferred_element_type=jnp.float32)
    summed = lax.psum_scatter(
        partial_out.astype(jnp.bfloat16), "ffn", scatter_dimension=2, tiled=True
    )
    returned = lax.all_to_all(summed, "expert", split_axis=0, concat_axis=0, tiled=True)
    mixed = jnp.dot(
        combine,
        returned.reshape(expert_count * capacity, -1).astype(jnp.float32),
        precision=lax.Precision.HIGHEST,
    )
    return (hidden + mixed).astype(jnp.bfloat16)


def solution(mesh):
    placed = (
        P(("expert", "ffn"), None),
        P(("expert", "ffn"), None),
        P(("expert", "ffn"), None),
        P(("expert", "ffn"), None, None),
        P(("expert", "ffn"), None, None),
        P(("expert", "ffn")),
        P("expert", "ffn"),
        P(None, "ffn"),
        P("ffn"),
        P("ffn", None),
        P("expert", None, "ffn"),
        P("expert", None, "ffn"),
        P("expert", "ffn", None),
        P("expert", None),
    )
    return jax.shard_map(
        local, mesh=mesh, in_specs=placed, out_specs=P("expert", "ffn"), check_vma=False
    )
```

profile of v0, /device:TPU:1, one launch (start us, length us, event | category | flops | bytes accessed | tf_op | source)
XLA Modules:
  0.0 292.3 jit_solution(4091025188030923789)
XLA Ops:
  6.5 1.4 reduce_max.18
  8.6 0.8 reshape.73
  9.5 0.7 reshape.91
  10.2 0.1 fusion.56
  10.3 6.2 %copy.47 = bf16[4,512,1024]{1,2,0:T(8,128)(2,1)} copy(bf16[4,512,1024]{2,1,0:T(8,128)(2,1)} %param.19) | data formatting | bytes 8388608 | tf_op args[3]
  16.5 6.2 %copy.48 = bf16[4,512,1024]{1,2,0:T(8,128)(2,1)} copy(bf16[4,512,1024]{2,1,0:T(8,128)(2,1)} %param.20) | data formatting | bytes 8388608 | tf_op args[4]
  22.8 0.0 copy-done.2
  22.8 0.0 copy-start.1
  22.9 9.4 %while.14 = (s32[]{:T(128)}, f32[4,8,4]{2,1,0:T(8,128)S(1)}, f32[4,8,4]{2,1,0:T(8,128)S(1)}, f32[4,8,4,128]{3,2,1,0:T(4,128)S(1)}, s32[]{:T(128)}, /*index=5*/s3...) while((s32[]{:T(128)}, f32[4,8,4]{2,1,0:T(8,128)S(1)}, ...), condition=%wide.region_4.5_spmd, body=%wide.region_1.4_spmd.sunk | while | flops 17106436 | bytes 4765895 | solution.py:66
  22.9 0.1 broadcast_compare_fusion.2
  23.0 2.1 fusion.77
  25.0 0.2 fusion.78
  25.3 2.3 fusion.79
  27.6 0.1 broadcast_compare_fusion.2
  27.7 2.1 fusion.77
  29.7 0.2 fusion.78
  30.0 2.3 fusion.79
  32.3 0.0 copy-start.5
  32.3 0.0 copy-start.6
  32.3 0.0 copy-start.3
  32.3 0.1 divide_convert_fusion
  32.5 19.6 %all-gather = bf16[16,4,4096]{2,1,0:T(4,128)(2,1)S(1)} all-gather(bf16[1,4,4096]{2,1,0:T(4,128)(2,1)S(1)} %reshape.82), channel_id=1, replica_groups=mesh['expert'=8,'ffn'=16] {'ffn'}, dimensions={0}, use_global_device_ids=true | all-gather | bytes 557056 | tf_op jit(solution)/shard_map/all_gather | solution.py:88
  52.0 0.1 reshape.83
  52.2 0.6 multiply_reduce_fusion
  52.8 30.9 %psum.14 = f32[64]{0:T(128)S(1)} all-reduce(f32[64]{0:T(128)S(1)} %get-tuple-element.118), channel_id=1, replica_groups=mesh['expert'=8,'ffn'=16] {'ffn'}, use_global_device_ids=true, to_apply=%region_8.9 | all-reduce | flops 64 | bytes 512 | tf_op jit(solution)/shard_map/psum | solution.py:94
  83.7 0.0 copy-done.6
  83.7 0.2 fusion.47
  83.9 28.5 %psum.15 = f32[64,8]{0,1:T(8,128)S(1)} all-reduce(f32[64,8]{0,1:T(8,128)S(1)} %fusion.47), channel_id=1, replica_groups=mesh['expert'=8,'ffn'=16] {'ffn'}, use_global_device_ids=true, to_apply=%region_9.10 | all-reduce | flops 512 | bytes 4096 | tf_op jit(solution)/shard_map/psum | solution.py:96
  112.4 0.0 copy-done.3
  112.4 0.1 copy.51
  112.5 0.1 eq.36
  112.7 0.1 fusion.45
  112.8 0.2 reduce_window_sum.11
  112.9 0.2 select_reduce_fusion.1
  113.1 0.1 reshape.78
  113.3 0.1 copy.52
  113.4 0.1 convert_reduce_fusion
  113.5 0.2 convolution_convert_fusion.1
  113.7 30.9 %all_to_all.10 = bf16[8,32,256]{2,1,0:T(8,128)(2,1)} all-to-all(bf16[8,32,256]{2,1,0:T(8,128)(2,1)S(1)} %bitcast.46), channel_id=1, replica_groups=mesh['expert'=8,'ffn'=16] {'expert'}, dimensions={0} | all-to-all | bytes 262144 | tf_op jit(solution)/shard_map/all_to_all | solution.py:123
  144.6 0.0 all-gather.3.cloned.1.call-update
  144.6 0.0 reduce-scatter.2.cloned.1.call-start
  144.7 41.4 %all-gather.3.cloned.1.call-done = bf16[8,32,4096]{2,1,0:T(8,128)(2,1)} async-done(((bf16[8,32,256]{2,1,0:T(8,128)(2,1)}), bf16[8,32,4096]{2,1,0:T(8,128)(2,1)}) %all-gather.3.cloned.1.call-update) | async-done | bytes 2097168 | tf_op jit(solution)/shard_map/all_gather | solution.py:122
  186.1 4.1 %fusion.28 = f32[8,32,512]{2,1,0:T(8,128)S(1)} fusion(bf16[8,32,4096]{2,1,0:T(8,128)(2,1)} %all-gather.3.cloned.1.call-done, bf16[1,4096,512]{2,1,0:T(8,128)(2,1)} %param.26), kind=kOutput, calls=%fused_computation.25 | convolution fusion | flops 1073741824 | bytes 6815744 | tf_op jit(solution)/shard_map/eck,kf->ecf/dot_general | solution.py:128
  190.2 7.8 %convolution_convert_fusion = bf16[8,32,4096]{2,1,0:T(8,128)(2,1)} fusion(bf16[1,512,4096]{2,1,0:T(8,128)(2,1)} %param.28, bf16[8,32,4096]{2,1,0:T(8,128)(2,1)} %all-gather.3.cloned.1.call-done, bf16[1,4096,512]{2,1,0:T(8,128)(2,1)} %param.27, f32[8,32,512]{2,1,0:T(8,128)S(1)} %fusion.28), kind=kOutput, calls=%fused_computation.21 | convolution fusion | flops 2149318656 | bytes 13107200 | tf_op jit(solution)/shard_map/ecf,fd->ecd/dot_general | solution.py:131
  198.0 0.0 reduce-scatter.2.cloned.1.call-update
  198.0 74.6 %reduce-scatter.2.cloned.1.call-done = bf16[8,32,256]{2,1,0:T(8,128)(2,1)} async-done(((bf16[8,32,4096]{2,1,0:T(8,128)(2,1)}), bf16[8,32,256]{2,1,0:T(8,128)(2,1)}) %reduce-scatter.2.cloned.1.call-update) | async-done | bytes 131088 | tf_op jit(solution)/shard_map/reduce_scatter | solution.py:132
  272.7 12.0 %all_to_all.11 = bf16[8,32,256]{2,1,0:T(8,128)(2,1)S(1)} all-to-all(bf16[8,32,256]{2,1,0:T(8,128)(2,1)} %reduce-scatter.2.cloned.1.call-done), channel_id=1, replica_groups=mesh['expert'=8,'ffn'=16] {'expert'}, dimensions={0} | all-to-all | bytes 262144 | tf_op jit(solution)/shard_map/all_to_all | solution.py:135
  284.6 0.8 fusion.36
  (27 shorter events, 0.2 us)
Async XLA Ops:
  6.5 45.6 %copy-start = (bf16[4096,256]{1,0:T(8,128)(2,1)S(1)}, bf16[4096,256]{1,0:T(8,128)(2,1)}, u32[]{:S(2)}) copy-start(bf16[4096,256]{1,0:T(8,128)(2,1)} %param.23) | copy-start | bytes 6291460
  6.5 179.6 %all-gather.3.cloned.1.call-start = ((), (), s32[]{:S(2)}) async-start(), calls=%async_computation.3 | async-start | bytes 2228224 | tf_op jit(solution)/shard_map/all_gather | solution.py:122
  16.5 6.2 %copy-start.4 = (bf16[4,1024]{1,0:T(4,128)(2,1)S(1)}, bf16[4,1024]{1,0:T(4,128)(2,1)}, u32[]{:S(2)}) copy-start(bf16[4,1024]{1,0:T(4,128)(2,1)} %param.18) | copy-start | bytes 24580
  16.5 6.3 %copy-start.2 = (s32[4]{0:T(128)S(1)}, s32[4]{0:T(128)}, u32[]{:S(2)}) copy-start(s32[4]{0:T(128)} %param.21) | copy-start | bytes 52
  22.8 29.3 %copy-start.1 = (bf16[64,256]{1,0:T(8,128)(2,1)S(1)}, bf16[64,256]{1,0:T(8,128)(2,1)}, u32[]{:S(2)}) copy-start(bf16[64,256]{1,0:T(8,128)(2,1)} %param.22) | copy-start | bytes 98308
  32.3 51.4 %copy-start.5 = (f32[256,8]{0,1:T(8,128)S(1)}, f32[256,8]{0,1:T(8,128)}, u32[]{:S(2)}) copy-start(f32[256,8]{0,1:T(8,128)} %param.25) | copy-start | bytes 24580
  32.3 51.3 %copy-start.6 = (f32[256]{0:T(256)S(1)}, f32[256]{0:T(256)}, u32[]{:S(2)}) copy-start(f32[256]{0:T(256)} %param.24) | copy-start | bytes 3076
  32.3 80.1 %copy-start.3 = (s32[64,2]{0,1:T(2,128)S(1)}, s32[64,2]{0,1:T(2,128)}, u32[]{:S(2)}) copy-start(s32[64,2]{0,1:T(2,128)} %param.29) | copy-start | bytes 1540
  144.6 128.0 %reduce-scatter.2.cloned.1.call-start = ((), (), s32[]{:S(2)}) async-start(), calls=%async_computation.4 | async-start | bytes 2228224 | tf_op jit(solution)/shard_map/reduce_scatter | solution.py:132
Sparse Core Ops, SparseCore 0:
  144.8 41.3 all-gather.2
  198.1 74.4 reduce-scatter.1
where the time goes:
time: 293 us; the launch traced here: 292 us
  blocking collectives  122 us (42%)
  waiting for transfers between devices  116 us (40%)
  matrix products  22.6 us (8%)
  local copies, waits for them, and re-layouts  14.6 us (5%)
  between operations  14.3 us (5%)
    reduce_scatter x1, waiting for transfers between devices, local(): lax.psum_scatter(partial_out.astype(jnp.bfloat16), 'ffn', scatter_dimensi...  74.6 us
    all_gather x1, waiting for transfers between devices, local(): lax.all_gather(lax.all_to_all(share_rows, 'expert', split_axis=0, concat_...  41.4 us
    all_to_all x1, blocking collectives, local(): lax.all_to_all(share_rows, 'expert', split_axis=0, concat_axis=0, tiled=T...  30.9 us
    psum x1, blocking collectives, local(): square_sum = lax.psum(square_part, 'ffn')  30.9 us
    psum x1, blocking collectives, local(): lax.psum(jnp.dot(scaled * inverse, router, precision=lax.Precision.HIGHES...  28.5 us
    all_gather x1, blocking collectives, local(): lax.all_gather(attended, 'ffn', axis=0, tiled=True)  19.6 us
    unnamed x20, local copies, waits for them, and re-layouts  12.7 us
    all_to_all x1, blocking collectives, local(): lax.all_to_all(summed, 'expert', split_axis=0, concat_axis=0, tiled=True)  12 us
  transfers between devices with their start and end apart: 2, of which 2 were waited for; matrix products, arithmetic and copies ran while one was open for 0% of the time, Pallas kernels for 0%

commit v1 on v0

--- a/solution.py
+++ b/solution.py
@@ -91,7 +91,11 @@
     )
     scaled = hidden * norm_gain
     square_part = jnp.sum(hidden * hidden, axis=-1)
-    square_sum = lax.psum(square_part, "ffn")
+    square_sum = square_part
+    for hop in (1, 2, 4, 8):
+        square_sum = square_sum + lax.ppermute(
+            square_sum, "ffn", [(dev, dev ^ hop) for dev in range(16)]
+        )
     inverse = lax.rsqrt(square_sum / D + EPSILON)[:, None]
     logits = lax.psum(jnp.dot(scaled * inverse, router, precision=lax.Precision.HIGHEST), "ffn")
     normed = (scaled * inverse).astype(jnp.bfloat16)

time: 293 us -> 273 us (0.932)
  blocking collectives: 122 us -> 90.7 us
  waiting for transfers between devices: 116 us -> 122 us
  starting transfers between devices: 0.04 us -> 4.69 us
    psum x1 -> x0, blocking collectives: 30.9 us -> none  [local(): square_sum = lax.psum(square_part, 'ffn')]
    ppermute x0 -> x4, waiting for transfers between devices: none -> 7.52 us  [local(): lax.ppermute(square_sum, 'ffn', [(dev, dev ^ hop) for dev in range(16)])]
    ppermute x0 -> x4, starting transfers between devices: none -> 4.64 us  [local(): lax.ppermute(square_sum, 'ffn', [(dev, dev ^ hop) for dev in range(16)])]
  transfers between devices with their start and end apart: 2 -> 6, of which waited for: 2 -> 6; matrix products, arithmetic and copies ran while one was open for 0% -> 0% of each run, Pallas kernels for 0% -> 0%
where the time goes in v1:
time: 273 us; the launch traced here: 272 us
  waiting for transfers between devices  122 us (45%)
  blocking collectives  90.7 us (33%)
  matrix products  22.5 us (8%)
  local copies, waits for them, and re-layouts  14.6 us (5%)
  between operations  14.3 us (5%)
  starting transfers between devices  4.69 us (2%)
  other arithmetic  2.77 us (1%)
    reduce_scatter x1, waiting for transfers between devices, local(): lax.psum_scatter(partial_out.astype(jnp.bfloat16), 'ffn', scatter_dimensi...  74.6 us
    all_gather x1, waiting for transfers between devices, local(): lax.all_gather(lax.all_to_all(share_rows, 'expert', split_axis=0, concat_...  40 us
    psum x1, blocking collectives, local(): lax.psum(jnp.dot(scaled * inverse, router, precision=lax.Precision.HIGHES...  30.9 us
    all_to_all x1, blocking collectives, local(): lax.all_to_all(share_rows, 'expert', split_axis=0, concat_axis=0, tiled=T...  28.2 us
    all_gather x1, blocking collectives, local(): lax.all_gather(attended, 'ffn', axis=0, tiled=True)  19.6 us
    unnamed x20, local copies, waits for them, and re-layouts  12.7 us
    all_to_all x1, blocking collectives, local(): lax.all_to_all(summed, 'expert', split_axis=0, concat_axis=0, tiled=True)  12 us
    dot_general x1, matrix products, local(): jnp.einsum('ecf,fd->ecd', inner, down_local, preferred_element_type=jnp.f...  7.79 us
  transfers between devices with their start and end apart: 6, of which 6 were waited for; matrix products, arithmetic and copies ran while one was open for 0% of the time, Pallas kernels for 0%

profile of v1, /device:TPU:1, one launch (start us, length us, event | category | flops | bytes accessed | tf_op | source)
XLA Modules:
  0.0 271.8 jit_solution(5912835144680152855)
XLA Ops:
  6.5 1.4 reduce_max.18
  8.6 0.8 reshape.73
  9.5 0.7 reshape.91
  10.2 0.1 fusion.56
  10.3 6.2 %copy.47 = bf16[4,512,1024]{1,2,0:T(8,128)(2,1)} copy(bf16[4,512,1024]{2,1,0:T(8,128)(2,1)} %param.19) | data formatting | bytes 8388608 | tf_op args[3]
  16.5 6.2 %copy.48 = bf16[4,512,1024]{1,2,0:T(8,128)(2,1)} copy(bf16[4,512,1024]{2,1,0:T(8,128)(2,1)} %param.20) | data formatting | bytes 8388608 | tf_op args[4]
  22.9 9.4 %while.14 = (s32[]{:T(128)}, f32[4,8,4]{2,1,0:T(8,128)S(1)}, f32[4,8,4]{2,1,0:T(8,128)S(1)}, f32[4,8,4,128]{3,2,1,0:T(4,128)S(1)}, s32[]{:T(128)}, /*index=5*/s3...) while((s32[]{:T(128)}, f32[4,8,4]{2,1,0:T(8,128)S(1)}, ...), condition=%wide.region_4.5_spmd, body=%wide.region_1.4_spmd.sunk | while | flops 17106436 | bytes 4765895 | solution.py:66
  22.9 0.1 broadcast_compare_fusion.2
  23.0 2.1 fusion.77
  25.0 0.2 fusion.78
  25.3 2.3 fusion.79
  27.6 0.1 broadcast_compare_fusion.2
  27.7 2.1 fusion.77
  29.7 0.2 fusion.78
  30.0 2.3 fusion.79
  32.3 0.1 divide_convert_fusion
  32.5 19.6 %all-gather = bf16[16,4,4096]{2,1,0:T(4,128)(2,1)S(1)} all-gather(bf16[1,4,4096]{2,1,0:T(4,128)(2,1)S(1)} %reshape.82), channel_id=1, replica_groups=mesh['expert'=8,'ffn'=16] {'ffn'}, dimensions={0}, use_global_device_ids=true | all-gather | bytes 557056 | tf_op jit(solution)/shard_map/all_gather | solution.py:88
  52.0 0.1 reshape.83
  52.2 0.6 multiply_reduce_fusion
  52.8 1.0 collective-permute-start
  53.8 0.1 copy.51
  53.9 0.1 eq.36
  54.0 1.5 collective-permute-done
  55.5 1.4 collective-permute-start.1
  56.9 0.1 fusion.45
  57.0 0.2 reduce_window_sum.11
  57.2 2.3 collective-permute-done.1
  59.5 0.6 collective-permute-start.2
  60.1 0.2 select_reduce_fusion.1
  60.2 0.1 reshape.78
  60.4 0.1 copy.52
  60.4 1.5 collective-permute-done.2
  61.9 1.7 collective-permute-start.3
  63.6 2.3 collective-permute-done.3
  65.8 0.2 fusion.47
  66.1 30.9 %psum.7 = f32[64,8]{0,1:T(8,128)S(1)} all-reduce(f32[64,8]{0,1:T(8,128)S(1)} %fusion.47), channel_id=1, replica_groups=mesh['expert'=8,'ffn'=16] {'ffn'}, use_global_device_ids=true, to_apply=%region_8.9 | all-reduce | flops 512 | bytes 4096 | tf_op jit(solution)/shard_map/psum | solution.py:100
  97.0 0.1 convert_reduce_fusion
  97.1 0.2 convolution_convert_fusion.1
  97.4 28.2 %all_to_all.10 = bf16[8,32,256]{2,1,0:T(8,128)(2,1)} all-to-all(bf16[8,32,256]{2,1,0:T(8,128)(2,1)S(1)} %bitcast.46), channel_id=1, replica_groups=mesh['expert'=8,'ffn'=16] {'expert'}, dimensions={0} | all-to-all | bytes 262144 | tf_op jit(solution)/shard_map/all_to_all | solution.py:127
  125.6 0.0 all-gather.3.cloned.1.call-update
  125.6 0.0 reduce-scatter.2.cloned.1.call-start
  125.7 40.0 %all-gather.3.cloned.1.call-done = bf16[8,32,4096]{2,1,0:T(8,128)(2,1)} async-done(((bf16[8,32,256]{2,1,0:T(8,128)(2,1)}), bf16[8,32,4096]{2,1,0:T(8,128)(2,1)}) %all-gather.3.cloned.1.call-update) | async-done | bytes 2097168 | tf_op jit(solution)/shard_map/all_gather | solution.py:126
  165.7 4.1 %fusion.28 = f32[8,32,512]{2,1,0:T(8,128)S(1)} fusion(bf16[8,32,4096]{2,1,0:T(8,128)(2,1)} %all-gather.3.cloned.1.call-done, bf16[1,4096,512]{2,1,0:T(8,128)(2,1)} %param.26), kind=kOutput, calls=%fused_computation.25 | convolution fusion | flops 1073741824 | bytes 6815744 | tf_op jit(solution)/shard_map/eck,kf->ecf/dot_general | solution.py:132
  169.7 7.8 %convolution_convert_fusion = bf16[8,32,4096]{2,1,0:T(8,128)(2,1)} fusion(bf16[1,512,4096]{2,1,0:T(8,128)(2,1)} %param.28, bf16[8,32,4096]{2,1,0:T(8,128)(2,1)} %all-gather.3.cloned.1.call-done, bf16[1,4096,512]{2,1,0:T(8,128)(2,1)} %param.27, f32[8,32,512]{2,1,0:T(8,128)S(1)} %fusion.28), kind=kOutput, calls=%fused_computation.21 | convolution fusion | flops 2149318656 | bytes 13107200 | tf_op jit(solution)/shard_map/ecf,fd->ecd/dot_general | solution.py:135
  177.5 0.0 reduce-scatter.2.cloned.1.call-update
  177.6 74.6 %reduce-scatter.2.cloned.1.call-done = bf16[8,32,256]{2,1,0:T(8,128)(2,1)} async-done(((bf16[8,32,4096]{2,1,0:T(8,128)(2,1)}), bf16[8,32,256]{2,1,0:T(8,128)(2,1)}) %reduce-scatter.2.cloned.1.call-update) | async-done | bytes 131088 | tf_op jit(solution)/shard_map/reduce_scatter | solution.py:136
  252.2 12.0 %all_to_all.11 = bf16[8,32,256]{2,1,0:T(8,128)(2,1)S(1)} all-to-all(bf16[8,32,256]{2,1,0:T(8,128)(2,1)} %reduce-scatter.2.cloned.1.call-done), channel_id=1, replica_groups=mesh['expert'=8,'ffn'=16] {'expert'}, dimensions={0} | all-to-all | bytes 262144 | tf_op jit(solution)/shard_map/all_to_all | solution.py:139
  264.2 0.8 fusion.36
  (37 shorter events, 0.2 us)
Async XLA Ops:
  6.5 45.6 %copy-start = (bf16[4096,256]{1,0:T(8,128)(2,1)S(1)}, bf16[4096,256]{1,0:T(8,128)(2,1)}, u32[]{:S(2)}) copy-start(bf16[4096,256]{1,0:T(8,128)(2,1)} %param.23) | copy-start | bytes 6291460
  6.5 159.1 %all-gather.3.cloned.1.call-start = ((), (), s32[]{:S(2)}) async-start(), calls=%async_computation.3 | async-start | bytes 2228224 | tf_op jit(solution)/shard_map/all_gather | solution.py:126
  16.5 6.2 %copy-start.4 = (bf16[4,1024]{1,0:T(4,128)(2,1)S(1)}, bf16[4,1024]{1,0:T(4,128)(2,1)}, u32[]{:S(2)}) copy-start(bf16[4,1024]{1,0:T(4,128)(2,1)} %param.18) | copy-start | bytes 24580
  16.5 6.3 %copy-start.2 = (s32[4]{0:T(128)S(1)}, s32[4]{0:T(128)}, u32[]{:S(2)}) copy-start(s32[4]{0:T(128)} %param.21) | copy-start | bytes 52
  22.8 29.3 %copy-start.1 = (bf16[64,256]{1,0:T(8,128)(2,1)S(1)}, bf16[64,256]{1,0:T(8,128)(2,1)}, u32[]{:S(2)}) copy-start(bf16[64,256]{1,0:T(8,128)(2,1)} %param.22) | copy-start | bytes 98308
  32.3 21.5 %copy-start.3 = (s32[64,2]{0,1:T(2,128)S(1)}, s32[64,2]{0,1:T(2,128)}, u32[]{:S(2)}) copy-start(s32[64,2]{0,1:T(2,128)} %param.29) | copy-start | bytes 1540
  32.3 33.5 %copy-start.5 = (f32[256,8]{0,1:T(8,128)S(1)}, f32[256,8]{0,1:T(8,128)}, u32[]{:S(2)}) copy-start(f32[256,8]{0,1:T(8,128)} %param.25) | copy-start | bytes 24580
  32.3 33.5 %copy-start.6 = (f32[256]{0:T(256)S(1)}, f32[256]{0:T(256)}, u32[]{:S(2)}) copy-start(f32[256]{0:T(256)} %param.24) | copy-start | bytes 3076
  52.8 2.8 %collective-permute-start = (f32[64]{0:T(128)S(1)}, f32[64]{0:T(128)S(1)}, u32[]{:S(2)}, u32[]{:S(2)}) collective-permute-start(f32[64]{0:T(128)S(1)} %get-tuple-element.118), channel_id=1, source_target_pairs={{0,1},{1,0},{2,3},{3,2},{4,5},{5,4},{6,7},{7,6},{8,9},{9,8},{10,11... | collective-permute-start | bytes 776 | tf_op jit(solution)/shard_map/ppermute | solution.py:96
  55.5 3.9 %collective-permute-start.1 = (f32[64]{0:T(128)S(1)}, f32[64]{0:T(128)S(1)}, u32[]{:S(2)}, u32[]{:S(2)}) collective-permute-start(f32[64]{0:T(128)S(1)} %add.70), channel_id=1, source_target_pairs={{0,2},{1,3},{2,0},{3,1},{4,6},{5,7},{6,4},{7,5},{8,10},{9,11},{10,... | collective-permute-start | bytes 776 | tf_op jit(solution)/shard_map/ppermute | solution.py:96
  59.5 2.4 collective-permute-start.2
  61.9 3.9 %collective-permute-start.3 = (f32[64]{0:T(128)S(1)}, f32[64]{0:T(128)S(1)}, u32[]{:S(2)}, u32[]{:S(2)}) collective-permute-start(f32[64]{0:T(128)S(1)} %add.72), channel_id=1, source_target_pairs={{0,8},{1,9},{2,10},{3,11},{4,12},{5,13},{6,14},{7,15},{8,0},{9,1},... | collective-permute-start | bytes 776 | tf_op jit(solution)/shard_map/ppermute | solution.py:96
  125.6 126.6 %reduce-scatter.2.cloned.1.call-start = ((), (), s32[]{:S(2)}) async-start(), calls=%async_computation.4 | async-start | bytes 2228224 | tf_op jit(solution)/shard_map/reduce_scatter | solution.py:136
Sparse Core Ops, SparseCore 0:
  125.8 39.8 all-gather.2
  177.7 74.4 reduce-scatter.1
